TPU v7x, 256 devices: a whole 4x4x8 slice. The times are simulated.
256 devices in a mesh: date: 64 (over x, y, z_lo, core), rng: 4 (over z_hi).
Axes of the slice: x: 4, y: 4, z: 8 (z_hi: 4, z_lo: 2; z = z_hi * 2 + z_lo), core: 2. Of those that a mesh axis runs over, the one named last changes fastest.
Arguments:
- slc_re: bfloat16 [64, 2048, 512], P('date', None, 'rng'), may hold values from -170 to 170
- slc_im: bfloat16 [64, 2048, 512], P('date', None, 'rng'), may hold values from -170 to 170
- ref_date: int32 [1], replicated, may hold values from 0 to 63
- gain: float32 [2048], replicated, may hold values from 0.25 to 2
- bperp: int32 [64], replicated, may hold values from -200 to 199
- tdays: int32 [64], replicated, may hold values from 0 to 1899
- mask: int32 [2048, 512], P(None, 'rng'), may hold values from 0 to 1, as said below
Outputs:
- periodogram: float32 [2048, 512, 256], P('date', 'rng')
Inputs may be any that keep to these rules, and one draw needn't show every extreme that they name: `mask`: each aligned block of 32 lines by 128 range columns holds exactly 1024 candidates.
All inputs are finite; a program needn't handle non-finite values.
Results may differ from a plain program's by a relative error of at most 0.0067.
Values may be sent and summed in bfloat16 or wider, within the bound.
No kernel may reach another device: no remote copies, remote signals or barrier semaphores. Data moves between devices by JAX's collectives and lax.ppermute only.
A program may use at most 64 MiB of HBM per device.

v0:
```python
import math
import jax
import jax.numpy as jnp
import numpy as np
from jax import lax
from jax.sharding import PartitionSpec as P

HGRID = 16
VGRID = 16
PHASE_Q = 1024


def dft_table(length):
    split = 64
    hi_count = length // split
    freq = jnp.arange(length, dtype=jnp.int32)[:, None]
    step = 2.0 * math.pi / length
    hi_ang = (freq * (split * jnp.arange(hi_count, dtype=jnp.int32)[None, :]) % length).astype(
        jnp.float32
    ) * step
    lo_ang = (freq * jnp.arange(split, dtype=jnp.int32)[None, :] % length).astype(
        jnp.float32
    ) * step
    hi_c, hi_s = (jnp.cos(hi_ang)[:, :, None], jnp.sin(hi_ang)[:, :, None])
    lo_c, lo_s = (jnp.cos(lo_ang)[:, None, :], jnp.sin(lo_ang)[:, None, :])
    cos_t = (hi_c * lo_c - hi_s * lo_s).reshape(length, length)
    sin_t = (hi_c * lo_s + hi_s * lo_c).reshape(length, length)
    table = jnp.concatenate([cos_t, sin_t], axis=1).astype(jnp.bfloat16)
    return lax.optimization_barrier(table)


def phase_tables(bperp, tdays):
    grid_points = jnp.arange(HGRID * VGRID, dtype=jnp.int32)
    height_step = grid_points // VGRID
    speed_step = grid_points % VGRID
    quanta = (
        bperp[:, None] * height_step[None, :] + tdays[:, None] * speed_step[None, :]
    ) % PHASE_Q
    angles = quanta.astype(jnp.float32) * (2.0 * math.pi / PHASE_Q)
    phase_re = jnp.cos(angles).astype(jnp.bfloat16)
    phase_im = jnp.sin(angles).astype(jnp.bfloat16)
    upper = jnp.concatenate([phase_re, -phase_im], axis=1)
    lower = jnp.concatenate([phase_im, phase_re], axis=1)
    return jnp.concatenate([upper, lower], axis=0)


def shards(slc_re, slc_im, ref_date, gain, bperp, tdays, mask):
    date_dev, lines, rg_dev = slc_re.shape
    assert date_dev == 1
    n_date = lax.axis_size("date")
    n_rng = lax.axis_size("rng")
    cols = rg_dev // n_date
    lines_dev = lines // n_date
    pixel_total = lines * rg_dev * n_rng
    me = lax.axis_index("date")
    f32 = jnp.float32
    own_re = slc_re[0]
    own_im = slc_im[0]
    wide_re = own_re.astype(f32)
    wide_im = own_im.astype(f32)
    local = jnp.sum(wide_re * wide_re + wide_im * wide_im)
    onehot = jnp.where(jnp.arange(n_date) == me, local, 0.0)
    date_sums = lax.psum(onehot, ("date", "rng"))
    scales = lax.rsqrt(date_sums / pixel_total + 1e-06)

    def to_date_rows(x):
        xt = x.T.reshape(cols, n_date, lines).transpose(1, 0, 2).reshape(n_date * cols, lines)
        return lax.all_to_all(xt, "date", split_axis=0, concat_axis=0, tiled=True)

    x_re = to_date_rows(own_re)
    x_im = to_date_rows(own_im)
    ref_index = ref_date[0]
    ref_scale = scales[ref_index]
    ref_re = lax.dynamic_slice_in_dim(x_re, ref_index * cols, cols, 0).astype(f32) * ref_scale
    ref_im = lax.dynamic_slice_in_dim(x_im, ref_index * cols, cols, 0).astype(f32) * ref_scale
    ref_re = jnp.tile(ref_re, (n_date, 1))
    ref_im = jnp.tile(ref_im, (n_date, 1))
    row_scale = jnp.repeat(scales, cols)[:, None]
    a_re = x_re.astype(f32) * row_scale
    a_im = x_im.astype(f32) * row_scale
    ifg_re = (a_re * ref_re + a_im * ref_im).astype(jnp.bfloat16)
    ifg_im = (a_im * ref_re - a_re * ref_im).astype(jnp.bfloat16)
    table = dft_table(lines)
    rows = n_date * cols
    stacked = jnp.concatenate([ifg_re, ifg_im], axis=0)
    fwd = jnp.dot(stacked, table, preferred_element_type=f32)
    spec_re = fwd[:rows, :lines] + fwd[rows:, lines:]
    spec_im = fwd[rows:, :lines] - fwd[:rows, lines:]
    weights = gain[None, :]
    held = jnp.concatenate(
        [(spec_re * weights).astype(jnp.bfloat16), (spec_im * weights).astype(jnp.bfloat16)], axis=0
    )
    back = jnp.dot(held, table, preferred_element_type=f32)
    filt_re = ((back[:rows, :lines] - back[rows:, lines:]) * (1.0 / lines)).astype(jnp.bfloat16)
    filt_im = ((back[:rows, lines:] + back[rows:, :lines]) * (1.0 / lines)).astype(jnp.bfloat16)

    def to_pixel_rows(x):
        got = lax.all_to_all(x.T, "date", split_axis=0, concat_axis=0, tiled=True)
        return got.reshape(n_date, lines_dev, rows).transpose(1, 0, 2).reshape(-1, rows)

    y_re = to_pixel_rows(filt_re)
    y_im = to_pixel_rows(filt_im)
    grid_size = HGRID * VGRID
    phase = phase_tables(bperp, tdays).reshape(2, n_date, 2, grid_size)
    eye = jnp.eye(cols, dtype=jnp.bfloat16)
    big = (phase[:, :, None, None, :, :] * eye[None, None, :, :, None, None]).reshape(
        2 * rows, cols * 2 * grid_size
    )
    ys = jnp.concatenate([y_re, y_im], axis=1)
    spectra = jnp.dot(ys, big, preferred_element_type=f32).reshape(-1, cols, 2, grid_size)
    peri_re = spectra[:, :, 0, :]
    peri_im = spectra[:, :, 1, :]
    wr = y_re.astype(f32)
    wi = y_im.astype(f32)
    sel = jnp.asarray(np.tile(np.eye(cols, dtype=np.float32), (n_date, 1)))
    pixel_power = jnp.dot(wr * wr + wi * wi, sel, precision=lax.Precision.HIGHEST) / n_date
    result = (peri_re * peri_re + peri_im * peri_im) / (n_date * jnp.maximum(pixel_power, 1.0))[
        :, :, None
    ]
    result = result.reshape(lines_dev, n_date, cols, grid_size).transpose(0, 2, 1, 3)
    result = result.reshape(lines_dev, cols * n_date, grid_size)
    mask_rows = lax.dynamic_slice_in_dim(mask, me * lines_dev, lines_dev, 0)
    return result * mask_rows.astype(f32)[:, :, None]


def solution(mesh):
    in_specs = (P("date", None, "rng"), P("date", None, "rng"), P(), P(), P(), P(), P(None, "rng"))
    out_specs = P("date", "rng", None)
    return jax.shard_map(shards, mesh=mesh, in_specs=in_specs, out_specs=out_specs, check_vma=False)
```

profile of v0, /device:TPU:1, one launch (start us, length us, event | category | flops | bytes accessed | tf_op | source)
XLA Modules:
  0.0 211.2 jit_solution(16790087384997871464)
XLA Ops:
  0.0 1.2 copy.24
  1.3 1.3 copy.25
  2.6 10.3 %all-to-all-start.1 = ((bf16[64,2,2048]{2,1,0:T(2,128)(2,1)}), bf16[64,2,2048]{2,1,0:T(2,128)(2,1)S(1)}, u32[]{:S(2)}, u32[]{:S(2)}) async-start(bf16[64,2,2048]{2,1,0:T(2,128)(2,1)} %copy.25), calls=%async_computation.1 | async-start | bytes 1048576 | tf_op jit(solution)/shard_map/all_to_all | solution.py:68
  14.0 2.0 fusion.38
  16.1 1.2 copy.22
  17.3 1.3 copy.23
  18.7 8.2 %subtract_convert_fusion = (bf16[2048,32,64]{0,2,1:T(8,128)(2,1)}, bf16[2048,32,64]{0,2,1:T(8,128)(2,1)}) fusion(f32[2048,64]{0,1:T(8,128)S(1)} %get-tuple-element.19, f32[2048,32]{0,1:T(8,128)S(1)} %get-tuple-element.16, f32[2048,64]{0,1:T(8,128)S(1)} %get-tuple-element.20, f32[2048,32]{0,1:T(8,128)S(1)} %get-tuple-element.15), kind=kLoop, calls=%fused_computation.2 | loop fusion | flops 33554432 | bytes 18350080 | tf_op jit(solution)/shard_map/convert.3
  26.9 8.8 %all-to-all-start = ((bf16[64,2,2048]{2,1,0:T(2,128)(2,1)}), bf16[64,2,2048]{2,1,0:T(2,128)(2,1)S(1)}, u32[]{:S(2)}, u32[]{:S(2)}) async-start(bf16[64,2,2048]{2,1,0:T(2,128)(2,1)} %copy.23), calls=%async_computation | async-start | bytes 1048576 | tf_op jit(solution)/shard_map/all_to_all | solution.py:68
  35.7 13.8 %pad_maximum_fusion = bf16[2048,4096]{0,1:T(8,128)(2,1)} fusion(bf16[2048,2048]{0,1:T(8,128)(2,1)} %bitcast.53, bf16[2048,2048]{0,1:T(8,128)(2,1)} %bitcast.52), kind=kLoop, calls=%fused_computation | loop fusion | flops 33554432 | bytes 33554432 | tf_op jit(solution)/shard_map/concatenate | solution.py:28
  51.7 80.4 %psum.7 = f32[64]{0:T(128)S(1)} all-reduce(f32[64]{0:T(128)S(1)} %compare_select_fusion), channel_id=1, replica_groups=mesh['date'=64,'rng'=4] {'date','rng'}, use_global_device_ids=true, to_apply=%region_1.2 | all-reduce | flops 64 | bytes 512 | tf_op jit(solution)/shard_map/psum | solution.py:63
  136.6 1.7 add_convert_fusion.1
  138.3 10.2 %fusion.11 = f32[256,4096]{1,0:T(8,128)} fusion(bf16[2048,4096]{0,1:T(8,128)(2,1)} %pad_maximum_fusion, bf16[128,2048]{1,0:T(8,128)(2,1)S(1)} %get-tuple-element.10, bf16[128,2048]{1,0:T(8,128)(2,1)S(1)} %get-tuple-element.9), kind=kOutput, calls=%fused_computation.23 | convolution fusion | flops 4297064448 | bytes 22020096 | tf_op jit(solution)/shard_map/dot_general | solution.py:86
  148.5 2.5 %fusion.10 = (bf16[128,2048]{1,0:T(8,128)(2,1)S(1)}, bf16[128,2048]{1,0:T(8,128)(2,1)S(1)}) fusion(f32[256,4096]{1,0:T(8,128)} %fusion.11, f32[2048]{0:T(1024)S(1)} %copy-done.2), kind=kLoop, calls=%fused_computation.22 | loop fusion | flops 1572864 | bytes 5251072 | tf_op jit(solution)/shard_map/convert_element_type | solution.py:91
  151.0 10.2 %fusion.15 = f32[256,4096]{1,0:T(8,128)} fusion(bf16[2048,4096]{0,1:T(8,128)(2,1)} %pad_maximum_fusion, bf16[128,2048]{1,0:T(8,128)(2,1)S(1)} %get-tuple-element.6, bf16[128,2048]{1,0:T(8,128)(2,1)S(1)} %get-tuple-element.5), kind=kOutput, calls=%fused_computation.27 | convolution fusion | flops 4297064448 | bytes 22020096 | tf_op jit(solution)/shard_map/dot_general | solution.py:93
  161.2 2.6 %fusion.30 = (bf16[2048,128]{0,1:T(8,128)(2,1)S(1)}, bf16[2048,128]{0,1:T(8,128)(2,1)S(1)}) fusion(f32[256,4096]{1,0:T(8,128)} %fusion.15), kind=kLoop, calls=%fused_computation.51 | loop fusion | flops 1572864 | bytes 5242880 | tf_op jit(solution)/shard_map/transpose | solution.py:98
  164.8 5.0 %all-to-all-start.3 = ((bf16[64,32,128]{2,1,0:T(8,128)(2,1)}), bf16[64,32,128]{2,1,0:T(8,128)(2,1)S(1)}, u32[]{:S(2)}, u32[]{:S(2)}) async-start(bf16[64,32,128]{2,1,0:T(8,128)(2,1)} %bitcast.17), calls=%async_computation.3 | async-start | bytes 1048576 | tf_op jit(solution)/shard_map/all_to_all | solution.py:98
  170.8 11.9 %all-to-all-done.3 = bf16[64,32,128]{2,1,0:T(8,128)(2,1)S(1)} async-done(((bf16[64,32,128]{2,1,0:T(8,128)(2,1)}), bf16[64,32,128]{2,1,0:T(8,128)(2,1)S(1)}, u32[]{:S(2)}, u32[]{:S(2)}) %all-to-all-start.3) | async-done | bytes 524320 | tf_op jit(solution)/shard_map/all_to_all | solution.py:98
  182.7 4.5 %all-to-all-start.2 = ((bf16[64,32,128]{2,1,0:T(8,128)(2,1)}), bf16[64,32,128]{2,1,0:T(8,128)(2,1)S(1)}, u32[]{:S(2)}, u32[]{:S(2)}) async-start(bf16[64,32,128]{2,1,0:T(8,128)(2,1)} %bitcast.13), calls=%async_computation.2 | async-start | bytes 1048576 | tf_op jit(solution)/shard_map/all_to_all | solution.py:98
  190.0 10.1 %all-to-all-done.2 = bf16[64,32,128]{2,1,0:T(8,128)(2,1)S(1)} async-done(((bf16[64,32,128]{2,1,0:T(8,128)(2,1)}), bf16[64,32,128]{2,1,0:T(8,128)(2,1)S(1)}, u32[]{:S(2)}, u32[]{:S(2)}) %all-to-all-start.2) | async-done | bytes 524320 | tf_op jit(solution)/shard_map/all_to_all | solution.py:98
  200.3 1.3 fusion.19
  201.6 2.6 %fusion = f32[2048,2,1,256]{3,0,2,1:T(8,128)} fusion(f32[2048,2,2,256]{3,0,2,1:T(8,128)S(1)} %fusion.19), kind=kLoop, calls=%fused_computation.4 | loop fusion | flops 3145728 | bytes 12582912 | tf_op jit(solution)/shard_map/add | solution.py:117
  204.2 1.1 fusion.2
  205.4 2.6 %divide_bitcast_fusion = f32[32,2,64,256]{3,2,0,1:T(8,128)S(1)} fusion(f32[32,64,2,256]{3,1,0,2:T(8,128)} %bitcast.54, f32[32,64,2]{1,0,2:T(8,128)S(1)} %div.33), kind=kLoop, calls=%fused_computation.7 | loop fusion | flops 1048576 | bytes 8404992 | tf_op jit(solution)/shard_map/transpose | solution.py:120
  208.5 2.6 %bitcast_multiply_fusion = f32[32,128,256]{2,1,0:T(8,128)} fusion(f32[32,2,64,256]{3,2,1,0:T(8,128)S(1)} %copy.31, f32[32,128]{1,0:T(8,128)S(1)} %dynamic-slice_convert_fusion), kind=kLoop, calls=%fused_computation.6 | loop fusion | flops 1048576 | bytes 8404992 | tf_op jit(solution)/shard_map/mul | solution.py:123
  (45 shorter events, 12.6 us)
Async XLA Ops:
  2.6 24.3 %all-to-all-start.1 = ((bf16[64,2,2048]{2,1,0:T(2,128)(2,1)}), bf16[64,2,2048]{2,1,0:T(2,128)(2,1)S(1)}, u32[]{:S(2)}, u32[]{:S(2)}) async-start(bf16[64,2,2048]{2,1,0:T(2,128)(2,1)} %copy.25), calls=%async_computation.1 | async-start | bytes 1048576 | tf_op jit(solution)/shard_map/all_to_all | solution.py:68
  26.9 106.3 %all-to-all-start = ((bf16[64,2,2048]{2,1,0:T(2,128)(2,1)}), bf16[64,2,2048]{2,1,0:T(2,128)(2,1)S(1)}, u32[]{:S(2)}, u32[]{:S(2)}) async-start(bf16[64,2,2048]{2,1,0:T(2,128)(2,1)} %copy.23), calls=%async_computation | async-start | bytes 1048576 | tf_op jit(solution)/shard_map/all_to_all | solution.py:68
  133.1 0.9 copy-start
  133.4 0.8 copy-start.1
  138.3 10.2 %copy-start.2 = (f32[2048]{0:T(1024)S(1)}, f32[2048]{0:T(1024)}, u32[]{:S(2)}) copy-start(f32[2048]{0:T(1024)} %param.11) | copy-start | bytes 24580
  161.2 26.1 %copy-start.3 = (s32[64]{0:T(128)S(1)}, s32[64]{0:T(128)}, u32[]{:S(2)}) copy-start(s32[64]{0:T(128)} %param.13) | copy-start | bytes 772
  161.2 26.1 %copy-start.4 = (s32[64]{0:T(128)S(1)}, s32[64]{0:T(128)}, u32[]{:S(2)}) copy-start(s32[64]{0:T(128)} %param.12) | copy-start | bytes 772
  164.8 17.9 %all-to-all-start.3 = ((bf16[64,32,128]{2,1,0:T(8,128)(2,1)}), bf16[64,32,128]{2,1,0:T(8,128)(2,1)S(1)}, u32[]{:S(2)}, u32[]{:S(2)}) async-start(bf16[64,32,128]{2,1,0:T(8,128)(2,1)} %bitcast.17), calls=%async_computation.3 | async-start | bytes 1048576 | tf_op jit(solution)/shard_map/all_to_all | solution.py:98
  182.7 17.4 %all-to-all-start.2 = ((bf16[64,32,128]{2,1,0:T(8,128)(2,1)}), bf16[64,32,128]{2,1,0:T(8,128)(2,1)S(1)}, u32[]{:S(2)}, u32[]{:S(2)}) async-start(bf16[64,32,128]{2,1,0:T(8,128)(2,1)} %bitcast.13), calls=%async_computation.2 | async-start | bytes 1048576 | tf_op jit(solution)/shard_map/all_to_all | solution.py:98
  201.6 2.6 %copy-start.5 = (f32[128,2]{1,0:T(8,128)S(1)}, f32[128,2]{1,0:T(8,128)}, u32[]{:S(2)}) copy-start(f32[128,2]{1,0:T(8,128)} %constant.105.clone) | copy-start | bytes 3076
where the time goes:
time: 212 us; the launch traced here: 211 us
  blocking collectives  80.4 us (38%)
  other arithmetic  43.8 us (21%)
  starting transfers between devices  28.7 us (14%)
  matrix products  22.8 us (11%)
  waiting for transfers between devices  22 us (10%)
  local copies, waits for them, and re-layouts  12.6 us (6%)
    psum x1, blocking collectives, shards(): date_sums = lax.psum(onehot, ('date', 'rng'))  80.4 us
    all_to_all x2, waiting for transfers between devices, to_pixel_rows(): got = lax.all_to_all(x.T, 'date', split_axis=0, concat_axis=0, tiled=True)  22 us
    all_to_all x2, starting transfers between devices, to_date_rows(): return lax.all_to_all(xt, 'date', split_axis=0, concat_axis=0, tiled=True)  19.2 us
    concatenate x1, other arithmetic, dft_table(): table = jnp.concatenate([cos_t, sin_t], axis=1).astype(jnp.bfloat16)  13.8 us
    dot_general x1, matrix products, shards(): fwd = jnp.dot(stacked, table, preferred_element_type=f32)  10.2 us
    dot_general x1, matrix products, shards(): back = jnp.dot(held, table, preferred_element_type=f32)  10.2 us
    all_to_all x2, starting transfers between devices, to_pixel_rows(): got = lax.all_to_all(x.T, 'date', split_axis=0, concat_axis=0, tiled=True)  9.56 us
    another operation x1, other arithmetic  8.21 us
  transfers between devices with their start and end apart: 4, of which 2 were waited for; matrix products, arithmetic and copies ran while one was open for 16% of the time, Pallas kernels for 0%

commit v1 on v0

--- a/solution.py
+++ b/solution.py
@@ -45,6 +45,10 @@
 
 
 def shards(slc_re, slc_im, ref_date, gain, bperp, tdays, mask):
+
+    def proceed_kinds(mesh_dim, x_local):
+        return jnp.sum(lax.all_gather(x_local, axis_name=mesh_dim), 0)
+
     date_dev, lines, rg_dev = slc_re.shape
     assert date_dev == 1
     n_date = lax.axis_size("date")
@@ -60,7 +64,7 @@
     wide_im = own_im.astype(f32)
     local = jnp.sum(wide_re * wide_re + wide_im * wide_im)
     onehot = jnp.where(jnp.arange(n_date) == me, local, 0.0)
-    date_sums = lax.psum(onehot, ("date", "rng"))
+    date_sums = proceed_kinds(("date", "rng"), onehot)
     scales = lax.rsqrt(date_sums / pixel_total + 1e-06)
 
     def to_date_rows(x):

time: 212 us -> 761 us (3.59)
  blocking collectives: 80.4 us -> 623 us
    all_gather x0 -> x1, blocking collectives: none -> 623 us  [proceed_kinds(): return jnp.sum(lax.all_gather(x_local, axis_name=mesh_dim), 0)]
    psum x1 -> x0, blocking collectives: 80.4 us -> none  [shards(): date_sums = lax.psum(onehot, ('date', 'rng'))]
  transfers between devices with their start and end apart: 4 -> 4, of which waited for: 2 -> 2; matrix products, arithmetic and copies ran while one was open for 16% -> 4% of each run, Pallas kernels for 0% -> 0%
where the time goes in v1:
time: 761 us; the launch traced here: 760 us
  blocking collectives  623 us (82%)
  other arithmetic  44.2 us (6%)
  starting transfers between devices  34.6 us (5%)
  matrix products  22.8 us (3%)
  waiting for transfers between devices  22 us (3%)
  local copies, waits for them, and re-layouts  12.6 us (2%)
    all_gather x1, blocking collectives, proceed_kinds(): return jnp.sum(lax.all_gather(x_local, axis_name=mesh_dim), 0)  623 us
    all_to_all x2, waiting for transfers between devices, to_pixel_rows(): got = lax.all_to_all(x.T, 'date', split_axis=0, concat_axis=0, tiled=True)  22 us
    all_to_all x2, starting transfers between devices, to_date_rows(): return lax.all_to_all(xt, 'date', split_axis=0, concat_axis=0, tiled=True)  19.2 us
    all_to_all x2, starting transfers between devices, to_pixel_rows(): got = lax.all_to_all(x.T, 'date', split_axis=0, concat_axis=0, tiled=True)  15.4 us
  transfers between devices with their start and end apart: 4, of which 2 were waited for; matrix products, arithmetic and copies ran while one was open for 4% of the time, Pallas kernels for 0%

profile of v1, /device:TPU:1, one launch (start us, length us, event | category | flops | bytes accessed | tf_op | source)
XLA Modules:
  0.0 760.3 jit_solution(3867804300220455670)
XLA Ops:
  0.0 1.2 copy.24
  1.3 1.3 copy.25
  2.6 10.3 %all-to-all-start.1 = ((bf16[64,2,2048]{2,1,0:T(2,128)(2,1)}), bf16[64,2,2048]{2,1,0:T(2,128)(2,1)S(1)}, u32[]{:S(2)}, u32[]{:S(2)}) async-start(bf16[64,2,2048]{2,1,0:T(2,128)(2,1)} %copy.25), calls=%async_computation.1 | async-start | bytes 1048576 | tf_op jit(solution)/shard_map/all_to_all | solution.py:72
  14.0 2.0 fusion.38
  16.1 1.2 copy.22
  17.3 1.3 copy.23
  18.7 8.2 %subtract_convert_fusion = (bf16[2048,32,64]{0,2,1:T(8,128)(2,1)}, bf16[2048,32,64]{0,2,1:T(8,128)(2,1)}) fusion(f32[2048,64]{0,1:T(8,128)S(1)} %get-tuple-element.19, f32[2048,32]{0,1:T(8,128)S(1)} %get-tuple-element.16, f32[2048,64]{0,1:T(8,128)S(1)} %get-tuple-element.20, f32[2048,32]{0,1:T(8,128)S(1)} %get-tuple-element.15), kind=kLoop, calls=%fused_computation.2 | loop fusion | flops 33554432 | bytes 18350080 | tf_op jit(solution)/shard_map/convert.3
  26.9 8.8 %all-to-all-start = ((bf16[64,2,2048]{2,1,0:T(2,128)(2,1)}), bf16[64,2,2048]{2,1,0:T(2,128)(2,1)S(1)}, u32[]{:S(2)}, u32[]{:S(2)}) async-start(bf16[64,2,2048]{2,1,0:T(2,128)(2,1)} %copy.23), calls=%async_computation | async-start | bytes 1048576 | tf_op jit(solution)/shard_map/all_to_all | solution.py:72
  35.7 13.8 %pad_maximum_fusion = bf16[2048,4096]{0,1:T(8,128)(2,1)} fusion(bf16[2048,2048]{0,1:T(8,128)(2,1)} %bitcast.55, bf16[2048,2048]{0,1:T(8,128)(2,1)} %bitcast.54), kind=kLoop, calls=%fused_computation | loop fusion | flops 33554432 | bytes 33554432 | tf_op jit(solution)/shard_map/concatenate | solution.py:28
  51.8 623.3 %all-gather = f32[256,1,64]{2,1,0:T(1,128)S(1)} all-gather(f32[1,1,64]{2,1,0:T(1,128)S(1)} %fusion.50), channel_id=1, replica_groups=mesh['date'=64,'rng'=4] {'date','rng'}, dimensions={0}, use_global_device_ids=true | all-gather | bytes 65792 | tf_op jit(solution)/shard_map/all_gather | solution.py:50
  679.9 1.7 add_convert_fusion.1
  681.6 10.2 %fusion.11 = f32[256,4096]{1,0:T(8,128)} fusion(bf16[2048,4096]{0,1:T(8,128)(2,1)} %pad_maximum_fusion, bf16[128,2048]{1,0:T(8,128)(2,1)S(1)} %get-tuple-element.10, bf16[128,2048]{1,0:T(8,128)(2,1)S(1)} %get-tuple-element.9), kind=kOutput, calls=%fused_computation.23 | convolution fusion | flops 4297064448 | bytes 22020096 | tf_op jit(solution)/shard_map/dot_general | solution.py:90
  691.8 2.5 fusion.10
  694.3 10.2 %fusion.15 = f32[256,4096]{1,0:T(8,128)} fusion(bf16[2048,4096]{0,1:T(8,128)(2,1)} %pad_maximum_fusion, bf16[128,2048]{1,0:T(8,128)(2,1)S(1)} %get-tuple-element.6, bf16[128,2048]{1,0:T(8,128)(2,1)S(1)} %get-tuple-element.5), kind=kOutput, calls=%fused_computation.27 | convolution fusion | flops 4297064448 | bytes 22020096 | tf_op jit(solution)/shard_map/dot_general | solution.py:97
  704.5 2.6 fusion.30
  708.1 10.9 %all-to-all-start.3 = ((bf16[64,32,128]{2,1,0:T(8,128)(2,1)}), bf16[64,32,128]{2,1,0:T(8,128)(2,1)S(1)}, u32[]{:S(2)}, u32[]{:S(2)}) async-start(bf16[64,32,128]{2,1,0:T(8,128)(2,1)} %bitcast.18), calls=%async_computation.3 | async-start | bytes 1048576 | tf_op jit(solution)/shard_map/all_to_all | solution.py:102
  720.0 11.9 %all-to-all-done.3 = bf16[64,32,128]{2,1,0:T(8,128)(2,1)S(1)} async-done(((bf16[64,32,128]{2,1,0:T(8,128)(2,1)}), bf16[64,32,128]{2,1,0:T(8,128)(2,1)S(1)}, u32[]{:S(2)}, u32[]{:S(2)}) %all-to-all-start.3) | async-done | bytes 524320 | tf_op jit(solution)/shard_map/all_to_all | solution.py:102
  731.9 4.5 all-to-all-start.2
  739.2 10.1 %all-to-all-done.2 = bf16[64,32,128]{2,1,0:T(8,128)(2,1)S(1)} async-done(((bf16[64,32,128]{2,1,0:T(8,128)(2,1)}), bf16[64,32,128]{2,1,0:T(8,128)(2,1)S(1)}, u32[]{:S(2)}, u32[]{:S(2)}) %all-to-all-start.2) | async-done | bytes 524320 | tf_op jit(solution)/shard_map/all_to_all | solution.py:102
  749.5 1.3 fusion.19
  750.8 2.6 fusion
  753.3 1.1 fusion.2
  754.6 2.6 divide_bitcast_fusion
  757.7 2.6 bitcast_multiply_fusion
  (46 shorter events, 13.0 us)
Async XLA Ops:
  2.6 24.3 %all-to-all-start.1 = ((bf16[64,2,2048]{2,1,0:T(2,128)(2,1)}), bf16[64,2,2048]{2,1,0:T(2,128)(2,1)S(1)}, u32[]{:S(2)}, u32[]{:S(2)}) async-start(bf16[64,2,2048]{2,1,0:T(2,128)(2,1)} %copy.25), calls=%async_computation.1 | async-start | bytes 1048576 | tf_op jit(solution)/shard_map/all_to_all | solution.py:72
  26.9 649.6 %all-to-all-start = ((bf16[64,2,2048]{2,1,0:T(2,128)(2,1)}), bf16[64,2,2048]{2,1,0:T(2,128)(2,1)S(1)}, u32[]{:S(2)}, u32[]{:S(2)}) async-start(bf16[64,2,2048]{2,1,0:T(2,128)(2,1)} %copy.23), calls=%async_computation | async-start | bytes 1048576 | tf_op jit(solution)/shard_map/all_to_all | solution.py:72
  676.4 0.9 copy-start
  676.7 0.8 copy-start.1
  681.6 10.2 %copy-start.2 = (f32[2048]{0:T(1024)S(1)}, f32[2048]{0:T(1024)}, u32[]{:S(2)}) copy-start(f32[2048]{0:T(1024)} %param.11) | copy-start | bytes 24580
  704.5 31.9 %copy-start.3 = (s32[64]{0:T(128)S(1)}, s32[64]{0:T(128)}, u32[]{:S(2)}) copy-start(s32[64]{0:T(128)} %param.13) | copy-start | bytes 772
  704.5 31.9 %copy-start.4 = (s32[64]{0:T(128)S(1)}, s32[64]{0:T(128)}, u32[]{:S(2)}) copy-start(s32[64]{0:T(128)} %param.12) | copy-start | bytes 772
  708.1 23.7 %all-to-all-start.3 = ((bf16[64,32,128]{2,1,0:T(8,128)(2,1)}), bf16[64,32,128]{2,1,0:T(8,128)(2,1)S(1)}, u32[]{:S(2)}, u32[]{:S(2)}) async-start(bf16[64,32,128]{2,1,0:T(8,128)(2,1)} %bitcast.18), calls=%async_computation.3 | async-start | bytes 1048576 | tf_op jit(solution)/shard_map/all_to_all | solution.py:102
  731.9 17.4 %all-to-all-start.2 = ((bf16[64,32,128]{2,1,0:T(8,128)(2,1)}), bf16[64,32,128]{2,1,0:T(8,128)(2,1)S(1)}, u32[]{:S(2)}, u32[]{:S(2)}) async-start(bf16[64,32,128]{2,1,0:T(8,128)(2,1)} %bitcast.14), calls=%async_computation.2 | async-start | bytes 1048576 | tf_op jit(solution)/shard_map/all_to_all | solution.py:102
  750.8 2.6 copy-start.5
